TPU v7x, 512 devices: a whole 4x4x16 slice. The times are simulated.
512 devices in a mesh: ctx: 32 (over z_hi, y, x), exp: 16 (over z_lo, core).
Axes of the slice: x: 4, y: 4, z: 16 (z_hi: 2, z_lo: 8; z = z_hi * 8 + z_lo), core: 2. Of those that a mesh axis runs over, the one named last changes fastest.
Arguments:
- hidden_in: bfloat16 [4096, 2880], P('ctx'), may hold values from -6 to 6
- query_input: bfloat16 [4096, 2048], P('ctx', 'exp'), may hold values from -16 to 16
- key_heads_input: bfloat16 [4096, 256], P('ctx'), may hold values from -16 to 16
- value_heads_input: bfloat16 [4096, 256], P('ctx'), may hold values from -6 to 6
- sink_logits: float32 [32], P('exp'), may hold values from 0 to 4
- out_proj: bfloat16 [2048, 2880], P('exp'), may hold values from -0.125 to 0.125
- norm_gain: float32 [2880], replicated, may hold values from 0.5 to 1.5
- expert_ids: int32 [4096, 4], P('ctx'), may hold values from 0 to 31, all different within a row; in each aligned block of 128 rows (0 to 127, 128 to 255, ...) at most 20 rows name the same one
- expert_gates: float32 [4096, 4], P('ctx'), may hold values from 0.1 to 1
- gate_up: bfloat16 [32, 2880, 2, 2880], P('ctx', None, None, 'exp'), may hold values from -0.109375 to 0.109375
- down_proj: bfloat16 [32, 2880, 2880], P('ctx', 'exp'), may hold values from -0.109375 to 0.109375
Outputs:
- layer_out: bfloat16 [4096, 2880], P('ctx', 'exp')
Inputs may be any that keep to these rules, and one draw needn't show every extreme that they name: `expert_ids`: each token names 4 different experts; within the 128 tokens of one device no expert is named by more than 20 tokens.
All inputs are finite; a program needn't handle non-finite values.
Results may differ from a plain program's by a relative error of at most 0.02.
Values may be sent and summed in bfloat16 or wider, within the bound.
No kernel may reach another device: no remote copies, remote signals or barrier semaphores. Data moves between devices by JAX's collectives and lax.ppermute only.
A program may use at most 64 MiB of HBM per device.

v0:
```python
import functools
import math
import jax
import jax.numpy as jnp
import numpy as np
from jax import lax
from jax.sharding import Mesh, PartitionSpec as P

D = 2880
QUERY_HEADS = 32
KEY_VALUE_HEADS = 4
HEAD_SIZE = 64
yarn_base = 150000.0
yarn_factor = 32.0
yarn_initial = 4096.0
beta_fast = 32.0
beta_slow = 1.0
neg_large = -1e30


def yarn_frequencies(head_dim):
    half_dim = head_dim // 2

    def correction(rotations):
        return (
            head_dim
            * math.log(yarn_initial / (rotations * 2.0 * math.pi))
            / (2.0 * math.log(yarn_base))
        )

    lower_dim = max(math.floor(correction(beta_fast)), 0)
    upper_dim = min(math.ceil(correction(beta_slow)), head_dim - 1)
    extrap_freq = 1.0 / yarn_base ** (np.arange(0, head_dim, 2) / head_dim)
    interp_freq = extrap_freq / yarn_factor
    ramp_part = np.clip((np.arange(half_dim) - lower_dim) / (upper_dim - lower_dim), 0.0, 1.0)
    extrap_share = 1.0 - ramp_part
    return (interp_freq * (1.0 - extrap_share) + extrap_freq * extrap_share).astype(np.float32)


def rotate_with_yarn(heads_in, token_positions):
    head_dim = heads_in.shape[-1]
    freqs = jnp.asarray(yarn_frequencies(head_dim))
    angles = token_positions.astype(jnp.float32)[:, None] * freqs[None, :]
    factor = 0.1 * math.log(yarn_factor) + 1.0
    cosine = (jnp.cos(angles) * factor)[:, None, :]
    sine = (jnp.sin(angles) * factor)[:, None, :]
    first_half = heads_in[..., : head_dim // 2]
    second_half = heads_in[..., head_dim // 2 :]
    return jnp.concatenate(
        [first_half * cosine - second_half * sine, second_half * cosine + first_half * sine],
        axis=-1,
    )


def route_slots(ids_block, n_experts):
    flat_ids = ids_block.reshape(-1)
    onehot = (flat_ids[:, None] == jnp.arange(n_experts, dtype=jnp.int32)[None, :]).astype(
        jnp.int32
    )
    ranks = jnp.cumsum(onehot, axis=0) - onehot
    return jnp.sum(ranks * onehot, axis=1).reshape(ids_block.shape)


CTX = ("zh", "y", "x")
EXP = ("zl", "c")


def per_device(
    hidden_in,
    query_input,
    key_heads_input,
    value_heads_input,
    sink_logits,
    out_proj,
    norm_gain,
    expert_ids,
    expert_gates,
    gate_up,
    down_proj,
    *,
    ctx_count,
    zl_count,
    c_count
):
    tok_rows = hidden_in.shape[0]
    exp_count = zl_count * c_count
    local_heads = query_input.shape[1] // HEAD_SIZE
    ctx_index = lax.axis_index(CTX)
    exp_index = lax.axis_index(EXP)
    token_positions = ctx_index * tok_rows + jnp.arange(tok_rows, dtype=jnp.int32)
    q_rot = rotate_with_yarn(
        query_input.astype(jnp.float32).reshape(tok_rows, local_heads, HEAD_SIZE), token_positions
    ).astype(jnp.bfloat16)
    shared_key_head = exp_index * local_heads // (QUERY_HEADS // KEY_VALUE_HEADS)
    key_block = lax.dynamic_slice_in_dim(key_heads_input, shared_key_head * HEAD_SIZE, HEAD_SIZE, 1)
    value_block = lax.dynamic_slice_in_dim(
        value_heads_input, shared_key_head * HEAD_SIZE, HEAD_SIZE, 1
    )
    key_rot = (
        rotate_with_yarn(
            key_block.astype(jnp.float32).reshape(tok_rows, 1, HEAD_SIZE), token_positions
        )
        .reshape(tok_rows, HEAD_SIZE)
        .astype(jnp.bfloat16)
    )
    key_value = jnp.concatenate([key_rot, value_block], axis=1)
    score_scale = 1.0 / math.sqrt(HEAD_SIZE)
    block_part = lax.all_gather(key_value, CTX, axis=0, tiled=True)
    run_max = jnp.broadcast_to(sink_logits[:, None], (local_heads, tok_rows))
    run_total = jnp.ones((local_heads, tok_rows), jnp.float32)
    key_count = block_part.shape[0]
    key_part = block_part[:, :HEAD_SIZE]
    value_part = block_part[:, HEAD_SIZE:].astype(jnp.float32)
    scores = (
        jnp.einsum("rhd,kd->hrk", q_rot, key_part, preferred_element_type=jnp.float32) * score_scale
    )
    key_pos = jnp.arange(key_count, dtype=jnp.int32)
    visible = token_positions[:, None] >= key_pos[None, :]
    scores = jnp.where(visible[None, :, :], scores, neg_large)
    new_max = jnp.maximum(run_max, jnp.max(scores, axis=2))
    weights = jnp.exp(scores - new_max[:, :, None])
    factor = jnp.exp(run_max - new_max)
    run_total = run_total * factor + jnp.sum(weights, axis=2)
    run_sum = jnp.einsum("hrk,kd->hrd", weights, value_part, precision=lax.Precision.HIGHEST)
    attended = (
        (run_sum / run_total[:, :, None])
        .transpose(1, 0, 2)
        .reshape(tok_rows, local_heads * HEAD_SIZE)
        .astype(jnp.bfloat16)
    )
    col_width = D // exp_count
    head_part = jnp.dot(attended, out_proj, preferred_element_type=jnp.float32).astype(jnp.bfloat16)
    head_part = head_part.reshape(tok_rows, zl_count, c_count, col_width).transpose(2, 1, 0, 3)
    head_part = lax.psum_scatter(head_part, "c", scatter_dimension=0, tiled=True)[0]
    head_cols = lax.psum_scatter(head_part, "zl", scatter_dimension=0, tiled=True)[0]
    residual_cols = lax.dynamic_slice_in_dim(hidden_in, exp_index * col_width, col_width, 1).astype(
        jnp.float32
    ) + head_cols.astype(jnp.float32)
    square_sum = lax.psum(jnp.sum(residual_cols * residual_cols, axis=1), EXP)
    gain_cols = lax.dynamic_slice_in_dim(norm_gain, exp_index * col_width, col_width, 0)
    normed_cols = (
        residual_cols * lax.rsqrt(square_sum / D + 1e-05)[:, None] * gain_cols[None, :]
    ).astype(jnp.bfloat16)
    exp_local = gate_up.shape[0]
    n_experts = exp_local * ctx_count
    top_count = expert_ids.shape[1]
    capacity = max(2, tok_rows * top_count * 5 // (4 * n_experts))
    slot_index = route_slots(expert_ids, n_experts)
    dest_row = expert_ids * capacity + slot_index
    spread_rows = jnp.broadcast_to(
        normed_cols[:, None, :], (tok_rows, top_count, col_width)
    ).reshape(tok_rows * top_count, col_width)
    send_rows = (
        jnp.zeros((n_experts * capacity, col_width), jnp.bfloat16)
        .at[dest_row.reshape(-1)]
        .set(spread_rows)
    )
    bucket_rows = ctx_count * capacity
    unit_count = gate_up.shape[-1]
    received = lax.all_to_all(
        send_rows.reshape(ctx_count, exp_local * capacity, col_width),
        CTX,
        split_axis=0,
        concat_axis=0,
        tiled=True,
    ).reshape(bucket_rows, col_width)
    gathered = lax.all_gather(received, "zl", axis=0, tiled=False)
    gathered = lax.all_gather(gathered, "c", axis=0, tiled=False)
    weights_flat = gate_up.reshape(zl_count, c_count, col_width, 2 * unit_count)
    gate_up_out = jnp.einsum(
        "czrk,zckf->rf", gathered, weights_flat, preferred_element_type=jnp.float32
    )
    gate_up_out = gate_up_out.reshape(bucket_rows, 2, unit_count)
    gate_value = gate_up_out[:, 0]
    up_value = gate_up_out[:, 1]
    activated = ((up_value + 1.0) * gate_value * jax.nn.sigmoid(1.702 * gate_value)).astype(
        jnp.bfloat16
    )
    down_local = down_proj.reshape(unit_count, zl_count, c_count, col_width)
    partial_value = jnp.einsum(
        "rf,fzcd->czrd", activated, down_local, preferred_element_type=jnp.float32
    ).astype(jnp.bfloat16)
    partial_value = lax.psum_scatter(partial_value, "c", scatter_dimension=0, tiled=True)[0]
    expert_cols = lax.psum_scatter(partial_value, "zl", scatter_dimension=0, tiled=True)[0]
    returned = lax.all_to_all(
        expert_cols.reshape(ctx_count, capacity, col_width),
        CTX,
        split_axis=0,
        concat_axis=0,
        tiled=True,
    )
    picked_rows = returned.reshape(n_experts * capacity, col_width)[dest_row]
    moe_cols = jnp.sum(expert_gates[:, :, None] * picked_rows.astype(jnp.float32), axis=1)
    return (residual_cols + moe_cols).astype(jnp.bfloat16)


def solution(mesh):
    ctx_count, exp_count = mesh.devices.shape
    zh, y, x = (mesh.devices.shape[0] // 16, 4, 4)
    c_count = 2
    zl_count = exp_count // c_count
    fine = Mesh(mesh.devices.reshape(zh, y, x, zl_count, c_count), ("zh", "y", "x", "zl", "c"))
    placed = (
        P(CTX, None),
        P(CTX, EXP),
        P(CTX, None),
        P(CTX, None),
        P(EXP),
        P(EXP, None),
        P(),
        P(CTX, None),
        P(CTX, None),
        P(CTX, None, None, EXP),
        P(CTX, EXP, None),
    )
    return jax.shard_map(
        functools.partial(per_device, ctx_count=ctx_count, zl_count=zl_count, c_count=c_count),
        mesh=fine,
        in_specs=placed,
        out_specs=P(CTX, EXP),
        check_vma=False,
    )
```

profile of v0, /device:TPU:32, one launch (start us, length us, event | category | flops | bytes accessed | tf_op | source)
XLA Modules:
  0.0 534.8 jit_solution(13582523231836904942)
XLA Ops:
  6.5 0.9 constant_dynamic-slice_fusion
  7.7 0.8 fusion.33
  8.5 0.6 pad_maximum_fusion
  9.2 0.8 copy.67
  10.1 0.8 fusion.39
  10.9 0.3 iota_compare_fusion
  11.3 113.0 %all-gather.5.cloned.1.call-done = bf16[4096,128]{0,1:T(8,128)(2,1)} async-done(((bf16[128,128]{0,1:T(8,128)(2,1)}), bf16[4096,128]{0,1:T(8,128)(2,1)}) %all-gather.5.cloned.1.call-update) | async-done | bytes 1048592 | tf_op jit(solution)/shard_map/all_gather | solution.py:108
  124.3 2.0 fusion.45
  126.4 0.6 fusion.2
  127.0 2.1 fusion.13
  129.1 0.3 convolution_convert_fusion
  129.4 0.1 reshape.307
  129.6 1.1 copy.69
  130.7 0.1 copy.73
  130.8 0.1 eq.29
  130.9 0.1 eq.25
  131.1 16.4 %reduce-scatter.11.cloned.1.call-done = bf16[1,8,128,180]{2,1,3,0:T(8,128)(2,1)} async-done(((bf16[2,8,128,180]{2,1,3,0:T(8,128)(2,1)}), bf16[1,8,128,180]{2,1,3,0:T(8,128)(2,1)}) %reduce-scatter.11.cloned.1.call-update) | async-done | bytes 368656 | tf_op jit(solution)/shard_map/reduce_scatter | solution.py:134
  147.5 1.8 copy.70
  149.3 0.8 constant_dynamic-slice_fusion.2
  150.1 0.1 copy.96
  150.2 0.8 dynamic_slice.15
  151.0 1.1 reduce-window.6
  152.2 0.2 slice_reduce_fusion
  152.4 0.1 fusion.24
  152.5 0.1 reshape.309
  152.7 0.1 copy.77
  152.9 0.1 reshape.310
  153.0 55.7 %reduce-scatter.15.cloned.1.call-done = bf16[1,128,180]{1,2,0:T(8,128)(2,1)} async-done(((bf16[8,128,180]{1,2,0:T(8,128)(2,1)}), bf16[1,128,180]{1,2,0:T(8,128)(2,1)}) %reduce-scatter.15.cloned.1.call-update) | async-done | bytes 46096
  208.7 0.9 copy.71
  209.6 0.1 multiply_reduce_fusion.1
  209.7 44.4 %psum.7 = f32[128]{0:T(128)S(1)} all-reduce(f32[128]{0:T(128)S(1)} %multiply_reduce_fusion.1), channel_id=1, replica_groups=mesh['zh'=2,'y'=4,'x'=4,'zl'=8,'c'=2] {'zl','c'}, use_global_device_ids=true, to_apply=%region_8.9 | all-reduce | flops 128 | bytes 1024 | tf_op jit(solution)/shard_map/psum | solution.py:139
  254.0 0.1 multiply_convert_fusion
  254.2 0.2 reshape.333
  254.4 2.4 scatter_custom_fusion
  256.9 30.0 %all_to_all.10 = bf16[32,20,180]{2,1,0:T(8,128)(2,1)S(1)} all-to-all(bf16[32,20,180]{2,1,0:T(8,128)(2,1)S(1)} %reshape.312), channel_id=1, replica_groups=mesh['zh'=2,'y'=4,'x'=4,'zl'=8,'c'=2] {'zh','y','x'}, dimensions={0} | all-to-all | bytes 460800 | tf_op jit(solution)/shard_map/all_to_all | solution.py:160
  286.9 0.1 all_gather_reshape.3
  287.1 0.8 copy.78
  288.0 62.0 %all-gather.7.cloned.1.call-done = bf16[8,640,180]{1,2,0:T(8,128)(2,1)} async-done(((bf16[1,640,180]{1,2,0:T(8,128)(2,1)}), bf16[8,640,180]{1,2,0:T(8,128)(2,1)}) %all-gather.7.cloned.1.call-update) | async-done | bytes 1843216 | tf_op jit(solution)/shard_map/all_gather | solution.py:167
  349.9 3.0 copy.79
  353.0 0.2 reduce-scatter.13.cloned.1.call-start
  353.2 1.8 copy.81
  355.0 9.8 %reshape.313 = bf16[8,2,180,360]{2,1,0,3:T(2,128)(2,1)} reshape(bf16[1,2880,2,180]{1,3,2,0:T(8,128)(2,1)S(1)} %copy.81) | data formatting | bytes 4147200 | tf_op jit(solution)/shard_map/reshape | solution.py:169
  364.8 6.4 %reshape.314 = bf16[180,8,2,180]{3,2,1,0:T(2,128)(2,1)S(1)} reshape(bf16[1,180,2880]{2,1,0:T(8,128)(2,1)} %param.23) | data formatting | bytes 2073600 | tf_op jit(solution)/shard_map/reshape | solution.py:179
  371.2 5.6 %all-gather.9.cloned.1.call-done = bf16[16,640,180]{1,0,2:T(8,128)(2,1)} async-done(((bf16[8,640,180]{1,0,2:T(8,128)(2,1)}), bf16[16,640,180]{1,0,2:T(8,128)(2,1)}) %all-gather.9.cloned.1.call-update) | async-done | bytes 3686416 | tf_op jit(solution)/shard_map/all_gather | solution.py:168
  376.8 3.0 copy.80
  379.8 3.0 fusion.8
  382.9 1.8 convert_bitcast_fusion
  384.7 2.6 copy.85
  387.3 0.3 reduce-scatter.17.cloned.1.call-start
  387.5 23.2 %reduce-scatter.13.cloned.1.call-done = bf16[1,8,640,180]{2,1,3,0:T(8,128)(2,1)} async-done(((bf16[2,8,640,180]{2,1,3,0:T(8,128)(2,1)}), bf16[1,8,640,180]{2,1,3,0:T(8,128)(2,1)}) %reduce-scatter.13.cloned.1.call-update) | async-done | bytes 1843216 | tf_op jit(solution)/shard_map/reduce_scatter | solution.py:183
  410.8 3.0 copy.86
  413.8 69.3 %reduce-scatter.17.cloned.1.call-done = bf16[1,640,180]{1,2,0:T(8,128)(2,1)} async-done(((bf16[8,640,180]{1,2,0:T(8,128)(2,1)}), bf16[1,640,180]{1,2,0:T(8,128)(2,1)}) %reduce-scatter.17.cloned.1.call-update) | async-done | bytes 230416
  483.1 1.1 copy.87
  484.2 0.8 reshape_squeeze.3
  485.0 17.0 %all-to-all-start.1 = ((bf16[32,20,180]{2,1,0:T(8,128)(2,1)}), bf16[32,20,180]{2,1,0:T(8,128)(2,1)S(1)}, u32[]{:S(2)}, u32[]{:S(2)}) async-start(bf16[32,20,180]{2,1,0:T(8,128)(2,1)} %reshape_squeeze.3), calls=%async_computation.3 | async-start | bytes 786432 | tf_op jit(solution)/shard_map/all_to_all | solution.py:185
  502.0 0.1 copy.88
  502.1 0.1 reshape.323
  502.2 0.1 copy.72
  502.3 22.2 %all-to-all-done.1 = bf16[32,20,180]{2,1,0:T(8,128)(2,1)S(1)} async-done(((bf16[32,20,180]{2,1,0:T(8,128)(2,1)}), bf16[32,20,180]{2,1,0:T(8,128)(2,1)S(1)}, u32[]{:S(2)}, u32[]{:S(2)}) %all-to-all-start.1) | async-done | bytes 230432 | tf_op jit(solution)/shard_map/all_to_all | solution.py:185
  524.5 0.1 reshape.315
  524.6 2.0 gather_fusion
  526.6 0.2 reshape.340
  526.8 0.4 multiply_reduce_fusion
  527.2 0.7 copy.89
  (44 shorter events, 1.0 us)
Async XLA Ops:
  6.5 122.5 %copy-start = (bf16[128,2880]{0,1:T(8,128)(2,1)S(1)}, bf16[128,2880]{0,1:T(8,128)(2,1)}, u32[]{:S(2)}) copy-start(bf16[128,2880]{0,1:T(8,128)(2,1)} %param.18) | copy-start | bytes 2211844
  6.5 119.7 %copy-start.5 = (f32[2]{0:T(128)S(1)}, f32[2]{0:T(128)}, u32[]{:S(2)}) copy-start(f32[2]{0:T(128)} %param.17) | copy-start | bytes 28
  6.5 117.7 %all-gather.5.cloned.1.call-start = ((), (), s32[]{:S(2)}) async-start(), calls=%async_computation.6 | async-start | bytes 1081344 | tf_op jit(solution)/shard_map/all_gather | solution.py:108
  9.2 138.3 %reduce-scatter.11.cloned.1.call-start = ((), (), s32[]{:S(2)}) async-start(), calls=%async_computation.7 | async-start | bytes 1105920 | tf_op jit(solution)/shard_map/reduce_scatter | solution.py:134
  124.3 2.7 copy-start.2
  129.1 1.6 copy-start.3
  130.7 78.0 %reduce-scatter.15.cloned.1.call-start = ((), (), s32[]{:S(2)}) async-start(), calls=%async_computation.11 | async-start | bytes 423936
  149.3 200.7 %all-gather.7.cloned.1.call-start = ((), (), s32[]{:S(2)}) async-start(), calls=%async_computation.8 | async-start | bytes 2119680 | tf_op jit(solution)/shard_map/all_gather | solution.py:167
  287.9 88.9 %all-gather.9.cloned.1.call-start = ((), (), s32[]{:S(2)}) async-start(), calls=%async_computation.10 | async-start | bytes 5529600 | tf_op jit(solution)/shard_map/all_gather | solution.py:168
  353.0 57.8 %reduce-scatter.13.cloned.1.call-start = ((), (), s32[]{:S(2)}) async-start(), calls=%async_computation.9 | async-start | bytes 5529600 | tf_op jit(solution)/shard_map/reduce_scatter | solution.py:183
  376.8 3.0 copy-start.1
  387.3 95.8 %reduce-scatter.17.cloned.1.call-start = ((), (), s32[]{:S(2)}) async-start(), calls=%async_computation.12 | async-start | bytes 2119680
  410.8 91.4 %copy-start.4 = (f32[128,4]{0,1:T(4,128)S(1)}, f32[128,4]{0,1:T(4,128)}, u32[]{:S(2)}) copy-start(f32[128,4]{0,1:T(4,128)} %param.21) | copy-start | bytes 6148
  485.0 39.5 %all-to-all-start.1 = ((bf16[32,20,180]{2,1,0:T(8,128)(2,1)}), bf16[32,20,180]{2,1,0:T(8,128)(2,1)S(1)}, u32[]{:S(2)}, u32[]{:S(2)}) async-start(bf16[32,20,180]{2,1,0:T(8,128)(2,1)} %reshape_squeeze.3), calls=%async_computation.3 | async-start | bytes 786432 | tf_op jit(solution)/shard_map/all_to_all | solution.py:185
Sparse Core Ops, SparseCore 0:
  11.4 112.7 all-gather.4
  130.8 16.6 reduce-scatter.10
  150.3 58.3 reduce-scatter.14
  288.1 61.8 all-gather.6
  353.1 23.7 all-gather.8
  387.4 23.3 reduce-scatter.12
  413.9 69.0 reduce-scatter.16
where the time goes:
time: 535 us
  waiting for transfers between devices  367 us (69%)
  blocking collectives  74.4 us (14%)
  local copies, waits for them, and re-layouts  46.9 us (9%)
  starting transfers between devices  17.6 us (3%)
  between operations  13.8 us (3%)
  matrix products  9.28 us (2%)
    unnamed x9, waiting for transfers between devices  125 us
    all_gather x1, waiting for transfers between devices, per_device(): block_part = lax.all_gather(key_value, CTX, axis=0, tiled=True)  113 us
    all_gather x1, waiting for transfers between devices, per_device(): gathered = lax.all_gather(received, 'zl', axis=0, tiled=False)  62 us
    psum x1, blocking collectives, per_device(): square_sum = lax.psum(jnp.sum(residual_cols * residual_cols, axis=1), EXP)  44.4 us
    all_to_all x1, blocking collectives, per_device(): lax.all_to_all(send_rows.reshape(ctx_count, exp_local * capacity, col_wid...  30 us
    reduce_scatter x1, waiting for transfers between devices, per_device(): lax.psum_scatter(partial_value, 'c', scatter_dimension=0, tiled=True)[0]  23.2 us
    all_to_all x1, waiting for transfers between devices, per_device(): lax.all_to_all(expert_cols.reshape(ctx_count, capacity, col_width), CTX,...  22.2 us
    all_to_all x1, starting transfers between devices, per_device(): lax.all_to_all(expert_cols.reshape(ctx_count, capacity, col_width), CTX,...  17 us
  transfers between devices with their start and end apart: 8, of which 8 were waited for; matrix products, arithmetic and copies ran while one was open for 5% of the time, Pallas kernels for 0%

commit v1 on v0

--- a/solution.py
+++ b/solution.py
@@ -136,7 +136,7 @@
     residual_cols = lax.dynamic_slice_in_dim(hidden_in, exp_index * col_width, col_width, 1).astype(
         jnp.float32
     ) + head_cols.astype(jnp.float32)
-    square_sum = lax.psum(jnp.sum(residual_cols * residual_cols, axis=1), EXP)
+    square_sum = lax.psum(lax.psum(jnp.sum(residual_cols * residual_cols, axis=1), "zl"), "c")
     gain_cols = lax.dynamic_slice_in_dim(norm_gain, exp_index * col_width, col_width, 0)
     normed_cols = (
         residual_cols * lax.rsqrt(square_sum / D + 1e-05)[:, None] * gain_cols[None, :]

time: 535 us -> 532 us (level)
  blocking collectives: 74.4 us -> 67 us
    psum x1 -> x2, blocking collectives: 44.4 us -> 35.5 us  [the longest x1 33.1 us: per_device(): lax.psum(jnp.sum(residual_cols * residual_cols, axis=1), 'zl')]
where the time goes in v1:
time: 532 us; the launch traced here: 531 us
  waiting for transfers between devices  371 us (70%)
  blocking collectives  67 us (13%)
  local copies, waits for them, and re-layouts  46.9 us (9%)
  starting transfers between devices  17.6 us (3%)
  between operations  13.8 us (3%)
  matrix products  9.28 us (2%)
    unnamed x9, waiting for transfers between devices  125 us
    all_gather x1, waiting for transfers between devices, per_device(): block_part = lax.all_gather(key_value, CTX, axis=0, tiled=True)  113 us
    all_gather x1, waiting for transfers between devices, per_device(): gathered = lax.all_gather(received, 'zl', axis=0, tiled=False)  65.6 us
    psum x1, blocking collectives, per_device(): lax.psum(jnp.sum(residual_cols * residual_cols, axis=1), 'zl')  33.1 us
    all_to_all x1, blocking collectives, per_device(): lax.all_to_all(send_rows.reshape(ctx_count, exp_local * capacity, col_wid...  31.4 us
    reduce_scatter x1, waiting for transfers between devices, per_device(): lax.psum_scatter(partial_value, 'c', scatter_dimension=0, tiled=True)[0]  23.2 us
    all_to_all x1, waiting for transfers between devices, per_device(): lax.all_to_all(expert_cols.reshape(ctx_count, capacity, col_width), CTX,...  22.2 us
    all_to_all x1, starting transfers between devices, per_device(): lax.all_to_all(expert_cols.reshape(ctx_count, capacity, col_width), CTX,...  16.9 us
  transfers between devices with their start and end apart: 8, of which 8 were waited for; matrix products, arithmetic and copies ran while one was open for 5% of the time, Pallas kernels for 0%

profile of v1, /device:TPU:32, one launch (start us, length us, event | category | flops | bytes accessed | tf_op | source)
XLA Modules:
  0.0 530.9 jit_solution(16450964898430038388)
XLA Ops:
  6.5 0.9 constant_dynamic-slice_fusion
  7.7 0.8 fusion.33
  8.5 0.6 pad_maximum_fusion
  9.2 0.8 copy.67
  10.1 0.8 fusion.39
  10.9 0.3 iota_compare_fusion
  11.3 113.0 %all-gather.5.cloned.1.call-done = bf16[4096,128]{0,1:T(8,128)(2,1)} async-done(((bf16[128,128]{0,1:T(8,128)(2,1)}), bf16[4096,128]{0,1:T(8,128)(2,1)}) %all-gather.5.cloned.1.call-update) | async-done | bytes 1048592 | tf_op jit(solution)/shard_map/all_gather | solution.py:108
  124.3 2.0 fusion.45
  126.4 0.6 fusion.2
  127.0 2.1 fusion.13
  129.1 0.3 convolution_convert_fusion
  129.4 0.1 reshape.307
  129.6 1.1 copy.69
  130.7 0.1 copy.73
  130.8 0.1 eq.29
  130.9 0.1 eq.25
  131.1 16.4 %reduce-scatter.11.cloned.1.call-done = bf16[1,8,128,180]{2,1,3,0:T(8,128)(2,1)} async-done(((bf16[2,8,128,180]{2,1,3,0:T(8,128)(2,1)}), bf16[1,8,128,180]{2,1,3,0:T(8,128)(2,1)}) %reduce-scatter.11.cloned.1.call-update) | async-done | bytes 368656 | tf_op jit(solution)/shard_map/reduce_scatter | solution.py:134
  147.5 1.8 copy.70
  149.3 0.8 constant_dynamic-slice_fusion.2
  150.1 0.1 copy.96
  150.2 0.8 dynamic_slice.15
  151.0 1.1 reduce-window.6
  152.2 0.2 slice_reduce_fusion
  152.4 0.1 fusion.24
  152.5 0.1 reshape.309
  152.7 0.1 copy.77
  152.9 0.1 reshape.310
  153.0 55.7 %reduce-scatter.15.cloned.1.call-done = bf16[1,128,180]{1,2,0:T(8,128)(2,1)} async-done(((bf16[8,128,180]{1,2,0:T(8,128)(2,1)}), bf16[1,128,180]{1,2,0:T(8,128)(2,1)}) %reduce-scatter.15.cloned.1.call-update) | async-done | bytes 46096
  208.7 0.9 copy.71
  209.6 0.1 multiply_reduce_fusion.1
  209.7 33.1 %psum.14 = f32[128]{0:T(128)S(1)} all-reduce(f32[128]{0:T(128)S(1)} %multiply_reduce_fusion.1), channel_id=1, replica_groups=mesh['zh'=2,'y'=4,'x'=4,'zl'=8,'c'=2] {'zl'}, use_global_device_ids=true, to_apply=%region_8.9 | all-reduce | flops 128 | bytes 1024 | tf_op jit(solution)/shard_map/psum | solution.py:139
  242.8 2.5 psum.15
  245.4 0.2 reshape.333
  245.6 2.4 scatter_custom_fusion
  248.1 31.4 %all_to_all.10 = bf16[32,20,180]{2,1,0:T(8,128)(2,1)S(1)} all-to-all(bf16[32,20,180]{2,1,0:T(8,128)(2,1)S(1)} %reshape.312), channel_id=1, replica_groups=mesh['zh'=2,'y'=4,'x'=4,'zl'=8,'c'=2] {'zh','y','x'}, dimensions={0} | all-to-all | bytes 460800 | tf_op jit(solution)/shard_map/all_to_all | solution.py:160
  279.5 0.1 all_gather_reshape.3
  279.6 0.8 copy.78
  280.5 65.6 %all-gather.7.cloned.1.call-done = bf16[8,640,180]{1,2,0:T(8,128)(2,1)} async-done(((bf16[1,640,180]{1,2,0:T(8,128)(2,1)}), bf16[8,640,180]{1,2,0:T(8,128)(2,1)}) %all-gather.7.cloned.1.call-update) | async-done | bytes 1843216 | tf_op jit(solution)/shard_map/all_gather | solution.py:167
  346.1 3.0 copy.79
  349.1 0.2 reduce-scatter.13.cloned.1.call-start
  349.4 1.8 copy.81
  351.2 9.8 %reshape.313 = bf16[8,2,180,360]{2,1,0,3:T(2,128)(2,1)} reshape(bf16[1,2880,2,180]{1,3,2,0:T(8,128)(2,1)S(1)} %copy.81) | data formatting | bytes 4147200 | tf_op jit(solution)/shard_map/reshape | solution.py:169
  360.9 6.4 %reshape.314 = bf16[180,8,2,180]{3,2,1,0:T(2,128)(2,1)S(1)} reshape(bf16[1,180,2880]{2,1,0:T(8,128)(2,1)} %param.23) | data formatting | bytes 2073600 | tf_op jit(solution)/shard_map/reshape | solution.py:179
  367.3 5.6 %all-gather.9.cloned.1.call-done = bf16[16,640,180]{1,0,2:T(8,128)(2,1)} async-done(((bf16[8,640,180]{1,0,2:T(8,128)(2,1)}), bf16[16,640,180]{1,0,2:T(8,128)(2,1)}) %all-gather.9.cloned.1.call-update) | async-done | bytes 3686416 | tf_op jit(solution)/shard_map/all_gather | solution.py:168
  373.0 3.0 copy.80
  376.0 3.0 fusion.8
  379.0 1.8 convert_bitcast_fusion
  380.9 2.6 copy.85
  383.4 0.3 reduce-scatter.17.cloned.1.call-start
  383.7 23.2 %reduce-scatter.13.cloned.1.call-done = bf16[1,8,640,180]{2,1,3,0:T(8,128)(2,1)} async-done(((bf16[2,8,640,180]{2,1,3,0:T(8,128)(2,1)}), bf16[1,8,640,180]{2,1,3,0:T(8,128)(2,1)}) %reduce-scatter.13.cloned.1.call-update) | async-done | bytes 1843216 | tf_op jit(solution)/shard_map/reduce_scatter | solution.py:183
  406.9 3.0 copy.86
  410.0 69.3 %reduce-scatter.17.cloned.1.call-done = bf16[1,640,180]{1,2,0:T(8,128)(2,1)} async-done(((bf16[8,640,180]{1,2,0:T(8,128)(2,1)}), bf16[1,640,180]{1,2,0:T(8,128)(2,1)}) %reduce-scatter.17.cloned.1.call-update) | async-done | bytes 230416
  479.3 1.1 copy.87
  480.4 0.8 reshape_squeeze.3
  481.2 16.9 %all-to-all-start.1 = ((bf16[32,20,180]{2,1,0:T(8,128)(2,1)}), bf16[32,20,180]{2,1,0:T(8,128)(2,1)S(1)}, u32[]{:S(2)}, u32[]{:S(2)}) async-start(bf16[32,20,180]{2,1,0:T(8,128)(2,1)} %reshape_squeeze.3), calls=%async_computation.3 | async-start | bytes 786432 | tf_op jit(solution)/shard_map/all_to_all | solution.py:185
  498.1 0.1 copy.88
  498.2 0.1 reshape.323
  498.4 0.1 copy.72
  498.5 22.2 %all-to-all-done.1 = bf16[32,20,180]{2,1,0:T(8,128)(2,1)S(1)} async-done(((bf16[32,20,180]{2,1,0:T(8,128)(2,1)}), bf16[32,20,180]{2,1,0:T(8,128)(2,1)S(1)}, u32[]{:S(2)}, u32[]{:S(2)}) %all-to-all-start.1) | async-done | bytes 230432 | tf_op jit(solution)/shard_map/all_to_all | solution.py:185
  520.6 0.1 reshape.315
  520.8 2.0 gather_fusion
  522.7 0.2 reshape.340
  522.9 0.4 multiply_reduce_fusion
  523.3 0.7 copy.89
  (45 shorter events, 1.1 us)
Async XLA Ops:
  6.5 122.5 %copy-start = (bf16[128,2880]{0,1:T(8,128)(2,1)S(1)}, bf16[128,2880]{0,1:T(8,128)(2,1)}, u32[]{:S(2)}) copy-start(bf16[128,2880]{0,1:T(8,128)(2,1)} %param.18) | copy-start | bytes 2211844
  6.5 119.7 %copy-start.5 = (f32[2]{0:T(128)S(1)}, f32[2]{0:T(128)}, u32[]{:S(2)}) copy-start(f32[2]{0:T(128)} %param.17) | copy-start | bytes 28
  6.5 117.7 %all-gather.5.cloned.1.call-start = ((), (), s32[]{:S(2)}) async-start(), calls=%async_computation.6 | async-start | bytes 1081344 | tf_op jit(solution)/shard_map/all_gather | solution.py:108
  9.2 138.3 %reduce-scatter.11.cloned.1.call-start = ((), (), s32[]{:S(2)}) async-start(), calls=%async_computation.7 | async-start | bytes 1105920 | tf_op jit(solution)/shard_map/reduce_scatter | solution.py:134
  124.3 2.7 copy-start.2
  129.1 1.6 copy-start.3
  130.7 78.0 %reduce-scatter.15.cloned.1.call-start = ((), (), s32[]{:S(2)}) async-start(), calls=%async_computation.11 | async-start | bytes 423936
  149.3 196.8 %all-gather.7.cloned.1.call-start = ((), (), s32[]{:S(2)}) async-start(), calls=%async_computation.8 | async-start | bytes 2119680 | tf_op jit(solution)/shard_map/all_gather | solution.py:167
  280.5 92.5 %all-gather.9.cloned.1.call-start = ((), (), s32[]{:S(2)}) async-start(), calls=%async_computation.10 | async-start | bytes 5529600 | tf_op jit(solution)/shard_map/all_gather | solution.py:168
  349.1 57.8 %reduce-scatter.13.cloned.1.call-start = ((), (), s32[]{:S(2)}) async-start(), calls=%async_computation.9 | async-start | bytes 5529600 | tf_op jit(solution)/shard_map/reduce_scatter | solution.py:183
  373.0 3.0 copy-start.1
  383.4 95.8 %reduce-scatter.17.cloned.1.call-start = ((), (), s32[]{:S(2)}) async-start(), calls=%async_computation.12 | async-start | bytes 2119680
  406.9 91.4 %copy-start.4 = (f32[128,4]{0,1:T(4,128)S(1)}, f32[128,4]{0,1:T(4,128)}, u32[]{:S(2)}) copy-start(f32[128,4]{0,1:T(4,128)} %param.21) | copy-start | bytes 6148
  481.2 39.4 %all-to-all-start.1 = ((bf16[32,20,180]{2,1,0:T(8,128)(2,1)}), bf16[32,20,180]{2,1,0:T(8,128)(2,1)S(1)}, u32[]{:S(2)}, u32[]{:S(2)}) async-start(bf16[32,20,180]{2,1,0:T(8,128)(2,1)} %reshape_squeeze.3), calls=%async_computation.3 | async-start | bytes 786432 | tf_op jit(solution)/shard_map/all_to_all | solution.py:185
Sparse Core Ops, SparseCore 0:
  11.4 112.7 all-gather.4
  130.8 16.6 reduce-scatter.10
  150.3 58.3 reduce-scatter.14
  280.6 65.4 all-gather.6
  349.2 23.7 all-gather.8
  383.6 23.3 reduce-scatter.12
  410.1 69.0 reduce-scatter.16
